TPU v7x, 512 devices: a whole 4x4x16 slice. The times are simulated.
512 devices in a mesh: ctx: 64 (over z_lo, y, core), wa: 8 (over z_hi, x).
Axes of the slice: x: 4, y: 4, z: 16 (z_hi: 2, z_lo: 8; z = z_hi * 8 + z_lo), core: 2. Of those that a mesh axis runs over, the one named last changes fastest.
Arguments:
- q_nope: bfloat16 [512, 8192], P('ctx', 'wa'), may hold values from -6 to 6
- q_rope: bfloat16 [512, 4096], P('ctx', 'wa'), may hold values from -100 to 100
- w_uk: bfloat16 [64, 128, 512], P('wa'), may hold values from -0.25 to 0.25
- w_uv: bfloat16 [64, 512, 128], P('wa'), may hold values from -0.25 to 0.25
- cache: bfloat16 [32768, 576], P('ctx'), may hold values from -16 to 16
- cache_scale: float32 [32768], P('ctx'), may hold values from 0.5 to 2, as said below
- new_latent: bfloat16 [512, 576], P('ctx'), may hold values from -16 to 16
- cache_doc: int32 [512], P('ctx'), may hold values from 0 to 15
- new_lengths: int32 [16], replicated, may hold values from 1 to 128, 512 in all
Outputs:
- attn_out: bfloat16 [512, 8192], P('ctx', 'wa')
Inputs may be any that keep to these rules, and one draw needn't show every extreme that they name: `cache_scale`: each scale is 0.5, 1 or 2.
All inputs are finite; a program needn't handle non-finite values.
Results may differ from a plain program's by a relative error of at most 0.0064.
Values may be sent and summed in bfloat16 or wider, within the bound.
No kernel may reach another device: no remote copies, remote signals or barrier semaphores. Data moves between devices by JAX's collectives and lax.ppermute only.
A program may use at most 64 MiB of HBM per device.

v0:
```python
import jax
import jax.numpy as jnp
from jax import lax
from jax.sharding import PartitionSpec as P


def doc_index(position, new_lengths):
    ends = jnp.cumsum(new_lengths)
    return jnp.sum((ends[None, :] <= position[:, None]).astype(jnp.int32), axis=1)


def absorb_rows(nope_rows, w_uk):
    row_count = nope_rows.shape[0]
    heads_dev, nope_dim, latent_dim = w_uk.shape
    shaped = nope_rows.reshape(row_count, heads_dev, nope_dim)
    absorbed = jnp.einsum("thn,hnl->thl", shaped, w_uk, preferred_element_type=jnp.float32)
    return absorbed.astype(jnp.bfloat16).reshape(row_count, heads_dev * latent_dim)


def body(q_nope, q_rope, w_uk, w_uv, cache, cache_scale, new_latent, cache_doc, new_lengths):
    tok_rows = q_nope.shape[0]
    heads_dev, nope_dim, latent_dim = w_uk.shape
    value_dim = w_uv.shape[2]
    rope_dim = q_rope.shape[1] // heads_dev
    shards = lax.axis_size("ctx")
    all_rows = tok_rows * shards
    my_index = lax.axis_index("ctx")
    score_scale = (nope_dim + rope_dim) ** (-0.5)
    own_lat = absorb_rows(q_nope, w_uk)
    all_lat, all_rope = (
        lax.all_gather(own_lat, "ctx", axis=0, tiled=True),
        lax.all_gather(q_rope, "ctx", axis=0, tiled=True),
    )
    query = jnp.concatenate(
        [
            all_lat.reshape(all_rows, heads_dev, latent_dim),
            all_rope.reshape(all_rows, heads_dev, rope_dim),
        ],
        axis=2,
    )
    dequant = (cache.astype(jnp.float32) * cache_scale[:, None]).astype(jnp.bfloat16)
    key_rows = jnp.concatenate([dequant, new_latent], axis=0)
    cache_len = cache.shape[0]
    block_len = cache_len // cache_doc.shape[0]
    query_pos = jnp.arange(all_rows, dtype=jnp.int32)
    query_doc = doc_index(query_pos, new_lengths)
    new_pos = my_index * tok_rows + jnp.arange(tok_rows, dtype=jnp.int32)
    key_doc = jnp.concatenate([jnp.repeat(cache_doc, block_len), doc_index(new_pos, new_lengths)])
    key_pos = jnp.concatenate([jnp.full((cache_len,), -1, dtype=jnp.int32), new_pos])
    allowed = (query_doc[:, None] == key_doc[None, :]) & (key_pos[None, :] <= query_pos[:, None])
    score = (
        jnp.einsum("qhl,kl->qhk", query, key_rows, preferred_element_type=jnp.float32) * score_scale
    )
    masked = jnp.where(allowed[:, None, :], score, -jnp.inf)
    local_max = jnp.max(masked, axis=2)
    shift = jnp.where(jnp.isfinite(local_max), local_max, jnp.zeros_like(local_max))
    weight = jnp.exp(masked - shift[:, :, None])
    totals = jnp.sum(weight, axis=2)
    weight_low = weight.astype(jnp.bfloat16)
    part_lat = jnp.einsum(
        "qhk,kl->qhl", weight_low, key_rows[:, :latent_dim], preferred_element_type=jnp.float32
    ).astype(jnp.bfloat16)
    numerator = jnp.einsum("qhl,hlv->qhv", part_lat, w_uv, preferred_element_type=jnp.float32)
    row_max = lax.pmax(local_max, "ctx")
    factor = jnp.exp(local_max - row_max)
    scaled = (numerator * factor[:, :, None]).reshape(all_rows, heads_dev * value_dim)
    own_numer, own_total = (
        lax.psum_scatter(scaled, "ctx", scatter_dimension=0, tiled=True),
        lax.psum_scatter(totals * factor, "ctx", scatter_dimension=0, tiled=True),
    )
    own_numer = own_numer.reshape(tok_rows, heads_dev, value_dim)
    result = own_numer / own_total[:, :, None]
    return result.astype(jnp.bfloat16).reshape(tok_rows, heads_dev * value_dim)


def solution(mesh):
    placed = (
        P("ctx", "wa"),
        P("ctx", "wa"),
        P("wa", None, None),
        P("wa", None, None),
        P("ctx", None),
        P("ctx"),
        P("ctx", None),
        P("ctx"),
        P(),
    )
    return jax.shard_map(
        body, mesh=mesh, in_specs=placed, out_specs=P("ctx", "wa"), check_vma=False
    )
```

profile of v0, /device:TPU:1, one launch (start us, length us, event | category | flops | bytes accessed | tf_op | source)
XLA Modules:
  0.0 1029.1 jit_solution(5514868261496968920)
XLA Ops:
  6.5 0.0 copy-start
  6.5 0.0 all-gather.2.cloned.1.call-start
  6.5 2.2 convolution_convert_fusion
  8.7 0.0 all-gather.2.cloned.1.call-update
  8.8 0.0 reduce-scatter.3.cloned.1.call-start
  8.8 0.7 copy.33
  9.6 0.1 reduce
  9.7 0.7 broadcast_in_dim.12
  10.4 0.1 reshape.99
  10.5 0.9 copy.36
  11.4 0.0 copy-start.2
  11.4 129.3 %all_gather.7 = bf16[512,512]{1,0:T(8,128)(2,1)S(1)} all-gather(bf16[8,512]{1,0:T(8,128)(2,1)} %param.10), channel_id=1, replica_groups=mesh['ctx'=64,'wa'=8] {'ctx'}, dimensions={0}, use_global_device_ids=true | all-gather | bytes 532480 | tf_op jit(solution)/shard_map/all_gather | solution.py:32
  140.7 0.2 copy.35
  140.9 0.2 convert_reduce_fusion.1
  141.1 0.1 convert_reduce_fusion
  141.2 0.3 fusion.23
  141.5 1.2 multiply_convert_fusion
  142.7 0.0 copy-start.1
  142.7 0.0 all-gather.2.cloned.1.call-done
  142.7 6.7 copy.34
  149.4 0.0 copy-done.2
  149.4 10.0 fusion
  159.4 0.0 copy-done.1
  159.4 408.2 %pmax.7 = f32[512,8]{0,1:T(8,128)S(1)} all-reduce(f32[512,8]{0,1:T(8,128)S(1)} %get-tuple-element.7), channel_id=1, replica_groups=mesh['ctx'=64,'wa'=8] {'ctx'}, use_global_device_ids=true, to_apply=%region_4.5 | all-reduce | flops 4096 | bytes 32768 | tf_op jit(solution)/shard_map/pmax | solution.py:64
  567.6 5.2 fusion.1
  572.7 0.0 copy-done
  572.8 7.8 bitcast_multiply_fusion
  580.5 1.9 copy.40
  582.4 0.0 reduce-scatter.3.cloned.1.call-update
  582.4 1.3 dynamic-slice
  584.4 419.0 %all-reduce.1 = f32[512,8]{0,1:T(8,128)S(1)} all-reduce(f32[512,8]{0,1:T(8,128)S(1)} %get-tuple-element.5), channel_id=3, replica_groups=mesh['ctx'=64,'wa'=8] {'ctx'}, use_global_device_ids=true, to_apply=%region_7.8.clone | all-reduce | flops 4096 | bytes 32768
  1003.4 0.1 constant_dynamic-slice_fusion
  1003.5 17.4 %reduce-scatter.3.cloned.1.call-done = f32[8,1024]{1,0:T(8,128)} async-done(((f32[512,1024]{1,0:T(8,128)}), f32[8,1024]{1,0:T(8,128)}) %reduce-scatter.3.cloned.1.call-update) | async-done | bytes 32784 | tf_op jit(solution)/shard_map/reduce_scatter | solution.py:68
  1020.8 1.4 fusion.31
  (6 shorter events, 0.1 us)
Async XLA Ops:
  6.5 566.2 %copy-start = (bf16[8,512,128]{2,1,0:T(8,128)(2,1)S(1)}, bf16[8,512,128]{2,1,0:T(8,128)(2,1)}, u32[]{:S(2)}) copy-start(bf16[8,512,128]{2,1,0:T(8,128)(2,1)} %param.12) | copy-start | bytes 3145732
  6.5 136.2 %all-gather.2.cloned.1.call-start = ((), (), s32[]{:S(2)}) async-start(), calls=%async_computation.1 | async-start | bytes 4259840 | tf_op jit(solution)/shard_map/all_gather | solution.py:31
  8.8 1012.1 %reduce-scatter.3.cloned.1.call-start = ((), (), s32[]{:S(2)}) async-start(), calls=%async_computation.2 | async-start | bytes 2129920 | tf_op jit(solution)/shard_map/reduce_scatter | solution.py:68
  11.4 138.0 %copy-start.2 = (bf16[8,576]{0,1:T(8,128)(2,1)}, bf16[8,576]{0,1:T(8,128)(2,1)S(1)}, u32[]{:S(2)}) copy-start(bf16[8,576]{0,1:T(8,128)(2,1)S(1)} %copy.36) | copy-start | bytes 27652
  142.7 16.7 %copy-start.1 = (bf16[512,576]{0,1:T(8,128)(2,1)}, bf16[512,576]{0,1:T(8,128)(2,1)S(1)}, u32[]{:S(2)}) copy-start(bf16[512,576]{0,1:T(8,128)(2,1)S(1)} %multiply_convert_fusion) | copy-start | bytes 1769476
Sparse Core Ops, SparseCore 0:
  9.5 128.3 all-gather.1
  582.5 438.2 reduce-scatter.2
where the time goes:
time: 1040 us; the launch traced here: 1030 us
  blocking collectives  956 us (92%)
  matrix products  19.9 us (2%)
  waiting for transfers between devices  17.4 us (2%)
  between operations  14.2 us (1%)
  local copies, waits for them, and re-layouts  12.5 us (1%)
    unnamed x1, blocking collectives  419 us
    pmax x1, blocking collectives, body(): row_max = lax.pmax(local_max, 'ctx')  408 us
    all_gather x1, blocking collectives, body(): lax.all_gather(q_rope, 'ctx', axis=0, tiled=True)  129 us
  transfers between devices with their start and end apart: 2, of which 1 were waited for; matrix products, arithmetic and copies ran while one was open for 1% of the time, Pallas kernels for 0%

commit v1 on v0

--- a/solution.py
+++ b/solution.py
@@ -14,7 +14,7 @@
     heads_dev, nope_dim, latent_dim = w_uk.shape
     shaped = nope_rows.reshape(row_count, heads_dev, nope_dim)
     absorbed = jnp.einsum("thn,hnl->thl", shaped, w_uk, preferred_element_type=jnp.float32)
-    return absorbed.astype(jnp.bfloat16).reshape(row_count, heads_dev * latent_dim)
+    return absorbed.astype(jnp.bfloat16)
 
 
 def body(q_nope, q_rope, w_uk, w_uv, cache, cache_scale, new_latent, cache_doc, new_lengths):
@@ -26,16 +26,13 @@
     all_rows = tok_rows * shards
     my_index = lax.axis_index("ctx")
     score_scale = (nope_dim + rope_dim) ** (-0.5)
-    own_lat = absorb_rows(q_nope, w_uk)
-    all_lat, all_rope = (
-        lax.all_gather(own_lat, "ctx", axis=0, tiled=True),
-        lax.all_gather(q_rope, "ctx", axis=0, tiled=True),
-    )
+    own_q = jnp.concatenate([q_nope, q_rope], axis=1)
+    all_q = lax.all_gather(own_q, "ctx", axis=0, tiled=True)
+    nope_width = heads_dev * nope_dim
+    all_lat = absorb_rows(all_q[:, :nope_width], w_uk)
+    all_rope = all_q[:, nope_width:]
     query = jnp.concatenate(
-        [
-            all_lat.reshape(all_rows, heads_dev, latent_dim),
-            all_rope.reshape(all_rows, heads_dev, rope_dim),
-        ],
+        [all_lat, all_rope.reshape(all_rows, heads_dev, rope_dim)],
         axis=2,
     )
     dequant = (cache.astype(jnp.float32) * cache_scale[:, None]).astype(jnp.bfloat16)
@@ -61,14 +58,16 @@
         "qhk,kl->qhl", weight_low, key_rows[:, :latent_dim], preferred_element_type=jnp.float32
     ).astype(jnp.bfloat16)
     numerator = jnp.einsum("qhl,hlv->qhv", part_lat, w_uv, preferred_element_type=jnp.float32)
-    row_max = lax.pmax(local_max, "ctx")
+    stats = lax.all_gather(jnp.concatenate([local_max, totals], axis=1), "ctx", axis=0, tiled=False)
+    row_max = jnp.max(stats[:, :, :heads_dev], axis=0)
     factor = jnp.exp(local_max - row_max)
     scaled = (numerator * factor[:, :, None]).reshape(all_rows, heads_dev * value_dim)
-    own_numer, own_total = (
-        lax.psum_scatter(scaled, "ctx", scatter_dimension=0, tiled=True),
-        lax.psum_scatter(totals * factor, "ctx", scatter_dimension=0, tiled=True),
-    )
+    own_numer = lax.psum_scatter(scaled, "ctx", scatter_dimension=0, tiled=True)
     own_numer = own_numer.reshape(tok_rows, heads_dev, value_dim)
+    own_stats = lax.dynamic_slice_in_dim(stats, my_index * tok_rows, tok_rows, axis=1)
+    own_max = lax.dynamic_slice_in_dim(row_max, my_index * tok_rows, tok_rows, axis=0)
+    own_factor = jnp.exp(own_stats[:, :, :heads_dev] - own_max[None])
+    own_total = jnp.sum(own_factor * own_stats[:, :, heads_dev:], axis=0)
     result = own_numer / own_total[:, :, None]
     return result.astype(jnp.bfloat16).reshape(tok_rows, heads_dev * value_dim)
 

time: 1040 us -> 728 us (0.70)
  blocking collectives: 956 us -> 0 us
  waiting for transfers between devices: 17.4 us -> 666 us
    unnamed x1 -> x0, blocking collectives: 419 us -> none
    reduce_scatter x1, waiting for transfers between devices: 17.4 us -> 427 us  [body(): own_numer = lax.psum_scatter(scaled, 'ctx', scatter_dimension=0, tiled=True)]
    pmax x1 -> x0, blocking collectives: 408 us -> none  [body(): row_max = lax.pmax(local_max, 'ctx')]
    all_gather x1 -> x2, waiting for transfers between devices: 0.02 us -> 239 us  [the longest x1 122 us: body(): all_q = lax.all_gather(own_q, 'ctx', axis=0, tiled=True)]
    all_gather x1 -> x0, blocking collectives: 129 us -> none  [body(): lax.all_gather(q_rope, 'ctx', axis=0, tiled=True)]
  transfers between devices with their start and end apart: 2 -> 3, of which waited for: 1 -> 3; matrix products, arithmetic and copies ran while one was open for 1% -> 1% of each run, Pallas kernels for 0% -> 0%
where the time goes in v1:
time: 728 us; the launch traced here: 718 us
  waiting for transfers between devices  666 us (91%)
  matrix products  16.3 us (2%)
  local copies, waits for them, and re-layouts  14.3 us (2%)
  between operations  13.2 us (2%)
  other arithmetic  8.3 us (1%)
    reduce_scatter x1, waiting for transfers between devices, body(): own_numer = lax.psum_scatter(scaled, 'ctx', scatter_dimension=0, tiled=True)  427 us
    all_gather x1, waiting for transfers between devices, body(): all_q = lax.all_gather(own_q, 'ctx', axis=0, tiled=True)  122 us
    all_gather x1, waiting for transfers between devices, body(): lax.all_gather(jnp.concatenate([local_max, totals], axis=1), 'ctx', axis=...  116 us
  transfers between devices with their start and end apart: 3, of which 3 were waited for; matrix products, arithmetic and copies ran while one was open for 1% of the time, Pallas kernels for 0%

profile of v1, /device:TPU:1, one launch (start us, length us, event | category | flops | bytes accessed | tf_op | source)
XLA Modules:
  0.0 718.2 jit_solution(12860980277982599046)
XLA Ops:
  6.5 0.0 copy-start
  6.5 0.0 all-gather.4.cloned.1.call-start
  6.5 1.4 pad_maximum_fusion.2
  8.0 0.0 all-gather.4.cloned.1.call-update
  8.0 0.0 all-gather.6.cloned.1.call-start
  8.0 0.7 copy.42
  8.8 0.1 reduce
  8.9 0.7 broadcast_in_dim.12
  9.7 0.1 reshape.99
  9.7 1.5 copy.47
  11.2 0.2 convert_reduce_fusion.1
  11.4 0.1 convert_reduce_fusion
  11.5 0.3 fusion.23
  11.8 2.0 multiply_convert_fusion
  13.8 122.1 %all-gather.4.cloned.1.call-done = bf16[512,1536]{1,0:T(8,128)(2,1)} async-done(((bf16[8,1536]{1,0:T(8,128)(2,1)}), bf16[512,1536]{1,0:T(8,128)(2,1)}) %all-gather.4.cloned.1.call-update) | async-done | bytes 1572880 | tf_op jit(solution)/shard_map/all_gather | solution.py:30
  135.9 1.3 slice.24
  137.2 0.5 copy.59
  137.7 0.0 copy-start.4
  137.7 1.1 slice.25
  138.9 1.0 copy.46
  139.9 0.0 copy-start.2
  139.9 0.0 copy-start.3
  139.9 0.0 copy-done
  139.9 1.3 convert_bitcast_fusion
  141.2 0.0 copy-done.4
  141.2 0.0 copy-done.2
  141.2 0.0 copy-done.3
  141.2 4.7 fusion
  145.9 0.0 copy-start.1
  145.9 1.7 fusion.1
  147.7 1.5 copy-done.1
  149.2 0.6 pad_maximum_fusion.1
  149.8 0.0 all-gather.6.cloned.1.call-update
  149.8 0.2 reduce-scatter.2.cloned.1.call-start
  150.0 116.5 %all-gather.6.cloned.1.call-done = f32[32768,16]{0,1:T(8,128)} async-done(((f32[512,16]{0,1:T(8,128)}), f32[32768,16]{0,1:T(8,128)}) %all-gather.6.cloned.1.call-update) | async-done | bytes 2097168 | tf_op jit(solution)/shard_map/all_gather | solution.py:61
  266.5 2.8 copy.60
  269.3 0.1 slice_reduce_fusion
  269.4 10.4 %bitcast_multiply_fusion = f32[512,8,128]{0,2,1:T(8,128)} fusion(bf16[8,512,128]{2,1,0:T(8,128)(2,1)} %param.12, f32[512,8,520]{0,2,1:T(8,128)} %copy-done.1, f32[512,8]{0,1:T(8,128)S(1)} %is-finite_select_fusion, pred[512,520]{0,1:T(8,128)(4,1)S(1)} %fusion.23, f32[512,8]{0,1:T(8,128)S(1)} %subtract_exponential_fusion.1, ...), kind=kOutput, calls=%fused_computation.17 | convolution fusion | flops 2730115072 | bytes 12563456 | tf_op jit(solution)/shard_map/qhl,hlv->qhv/dot_general | solution.py:60
  279.8 2.9 copy.51
  282.7 0.0 reduce-scatter.2.cloned.1.call-update
  282.8 0.1 constant_dynamic-slice_fusion
  282.8 0.2 fusion.31
  283.1 427.2 %reduce-scatter.2.cloned.1.call-done = f32[8,1024]{1,0:T(8,128)} async-done(((f32[512,1024]{1,0:T(8,128)}), f32[8,1024]{1,0:T(8,128)}) %reduce-scatter.2.cloned.1.call-update) | async-done | bytes 32784 | tf_op jit(solution)/shard_map/reduce_scatter | solution.py:65
  710.3 1.4 fusion.33
  (6 shorter events, 0.1 us)
Async XLA Ops:
  6.5 133.3 %copy-start = (bf16[8,128,512]{2,1,0:T(8,128)(2,1)S(1)}, bf16[8,128,512]{2,1,0:T(8,128)(2,1)}, u32[]{:S(2)}) copy-start(bf16[8,128,512]{2,1,0:T(8,128)(2,1)} %param.11) | copy-start | bytes 3145732
  6.5 129.3 %all-gather.4.cloned.1.call-start = ((), (), s32[]{:S(2)}) async-start(), calls=%async_computation.1 | async-start | bytes 1597440 | tf_op jit(solution)/shard_map/all_gather | solution.py:30
  8.0 258.5 %all-gather.6.cloned.1.call-start = ((), (), s32[]{:S(2)}) async-start(), calls=%async_computation.3 | async-start | bytes 2129920 | tf_op jit(solution)/shard_map/all_gather | solution.py:61
  137.7 3.4 copy-start.4
  139.9 1.3 copy-start.2
  139.9 1.3 copy-start.3
  145.9 3.3 copy-start.1
  149.8 560.5 %reduce-scatter.2.cloned.1.call-start = ((), (), s32[]{:S(2)}) async-start(), calls=%async_computation.2 | async-start | bytes 2129920 | tf_op jit(solution)/shard_map/reduce_scatter | solution.py:65
Sparse Core Ops, SparseCore 0:
  9.5 126.3 all-gather.3
  149.9 116.5 all-gather.5
  282.9 427.3 reduce-scatter.1

commit v2 on v1

--- a/solution.py
+++ b/solution.py
@@ -1,7 +1,10 @@
 import jax
 import jax.numpy as jnp
+import numpy as np
 from jax import lax
-from jax.sharding import PartitionSpec as P
+from jax.sharding import Mesh, PartitionSpec as P
+
+CTX_PARTS = ("cz", "cy", "cc")
 
 
 def doc_index(position, new_lengths):
@@ -17,17 +20,49 @@
     return absorbed.astype(jnp.bfloat16)
 
 
+def ctx_index():
+    index = lax.axis_index(CTX_PARTS[0])
+    for name in CTX_PARTS[1:]:
+        index = index * lax.axis_size(name) + lax.axis_index(name)
+    return index
+
+
+def gather_rows(x):
+    for name in reversed(CTX_PARTS):
+        x = lax.all_gather(x, name, axis=0, tiled=True)
+    return x
+
+
+def scatter_rows(x):
+    for name in CTX_PARTS:
+        x = lax.psum_scatter(x, name, scatter_dimension=0, tiled=True)
+    return x
+
+
+def merge_stats(stats, heads_dev):
+    for name in reversed(CTX_PARTS):
+        group = lax.all_gather(stats, name, axis=0, tiled=False)
+        peak = jnp.max(group[:, :, :heads_dev], axis=0)
+        shifted = jnp.where(jnp.isfinite(peak), peak, jnp.zeros_like(peak))
+        scale = jnp.exp(group[:, :, :heads_dev] - shifted[None])
+        total = jnp.sum(scale * group[:, :, heads_dev:], axis=0)
+        stats = jnp.concatenate([peak, total], axis=1)
+    return stats[:, :heads_dev], stats[:, heads_dev:]
+
+
 def body(q_nope, q_rope, w_uk, w_uv, cache, cache_scale, new_latent, cache_doc, new_lengths):
     tok_rows = q_nope.shape[0]
     heads_dev, nope_dim, latent_dim = w_uk.shape
     value_dim = w_uv.shape[2]
     rope_dim = q_rope.shape[1] // heads_dev
-    shards = lax.axis_size("ctx")
+    shards = 1
+    for name in CTX_PARTS:
+        shards = shards * lax.axis_size(name)
     all_rows = tok_rows * shards
-    my_index = lax.axis_index("ctx")
+    my_index = ctx_index()
     score_scale = (nope_dim + rope_dim) ** (-0.5)
     own_q = jnp.concatenate([q_nope, q_rope], axis=1)
-    all_q = lax.all_gather(own_q, "ctx", axis=0, tiled=True)
+    all_q = gather_rows(own_q)
     nope_width = heads_dev * nope_dim
     all_lat = absorb_rows(all_q[:, :nope_width], w_uk)
     all_rope = all_q[:, nope_width:]
@@ -58,32 +93,31 @@
         "qhk,kl->qhl", weight_low, key_rows[:, :latent_dim], preferred_element_type=jnp.float32
     ).astype(jnp.bfloat16)
     numerator = jnp.einsum("qhl,hlv->qhv", part_lat, w_uv, preferred_element_type=jnp.float32)
-    stats = lax.all_gather(jnp.concatenate([local_max, totals], axis=1), "ctx", axis=0, tiled=False)
-    row_max = jnp.max(stats[:, :, :heads_dev], axis=0)
+    row_max, row_total = merge_stats(jnp.concatenate([local_max, totals], axis=1), heads_dev)
     factor = jnp.exp(local_max - row_max)
     scaled = (numerator * factor[:, :, None]).reshape(all_rows, heads_dev * value_dim)
-    own_numer = lax.psum_scatter(scaled, "ctx", scatter_dimension=0, tiled=True)
-    own_numer = own_numer.reshape(tok_rows, heads_dev, value_dim)
-    own_stats = lax.dynamic_slice_in_dim(stats, my_index * tok_rows, tok_rows, axis=1)
-    own_max = lax.dynamic_slice_in_dim(row_max, my_index * tok_rows, tok_rows, axis=0)
-    own_factor = jnp.exp(own_stats[:, :, :heads_dev] - own_max[None])
-    own_total = jnp.sum(own_factor * own_stats[:, :, heads_dev:], axis=0)
+    own_numer = scatter_rows(scaled).reshape(tok_rows, heads_dev, value_dim)
+    own_total = lax.dynamic_slice_in_dim(row_total, my_index * tok_rows, tok_rows, axis=0)
     result = own_numer / own_total[:, :, None]
     return result.astype(jnp.bfloat16).reshape(tok_rows, heads_dev * value_dim)
 
 
 def solution(mesh):
+    ctx_shape = (8, 4, 2)
+    grid = np.asarray(mesh.devices).reshape(ctx_shape + (mesh.shape["wa"],))
+    fine = Mesh(grid, CTX_PARTS + ("wa",))
+    rows = CTX_PARTS
     placed = (
-        P("ctx", "wa"),
-        P("ctx", "wa"),
+        P(rows, "wa"),
+        P(rows, "wa"),
         P("wa", None, None),
         P("wa", None, None),
-        P("ctx", None),
-        P("ctx"),
-        P("ctx", None),
-        P("ctx"),
+        P(rows, None),
+        P(rows),
+        P(rows, None),
+        P(rows),
         P(),
     )
     return jax.shard_map(
-        body, mesh=mesh, in_specs=placed, out_specs=P("ctx", "wa"), check_vma=False
+        body, mesh=fine, in_specs=placed, out_specs=P(rows, "wa"), check_vma=False
     )

time: 728 us -> 310 us (0.43); the launches traced: 718 us -> 309 us
  waiting for transfers between devices: 666 us -> 183 us
  blocking collectives: 0 us -> 77.2 us
    reduce_scatter x1 -> x3, waiting for transfers between devices: 427 us -> 125 us  [scatter_rows(): x = lax.psum_scatter(x, name, scatter_dimension=0, tiled=True)]
    all_gather x2 -> x1, waiting for transfers between devices: 239 us -> 58 us  [gather_rows(): x = lax.all_gather(x, name, axis=0, tiled=True)]
    all_gather x0 -> x5, blocking collectives: none -> 77.2 us  [the longest x3 58.9 us: merge_stats(): group = lax.all_gather(stats, name, axis=0, tiled=False)]
  transfers between devices with their start and end apart: 3 -> 4, of which waited for: 3 -> 4; matrix products, arithmetic and copies ran while one was open for 1% -> 2% of each run, Pallas kernels for 0% -> 0%
where the time goes in v2:
time: 310 us; the launch traced here: 309 us
  waiting for transfers between devices  183 us (59%)
  blocking collectives  77.2 us (25%)
  matrix products  15.1 us (5%)
  between operations  13.4 us (4%)
  local copies, waits for them, and re-layouts  12.5 us (4%)
  other arithmetic  7.81 us (3%)
    reduce_scatter x3, waiting for transfers between devices, scatter_rows(): x = lax.psum_scatter(x, name, scatter_dimension=0, tiled=True)  125 us
    all_gather x3, blocking collectives, merge_stats(): group = lax.all_gather(stats, name, axis=0, tiled=False)  58.9 us
    all_gather x1, waiting for transfers between devices, gather_rows(): x = lax.all_gather(x, name, axis=0, tiled=True)  58 us
    all_gather x2, blocking collectives, gather_rows(): x = lax.all_gather(x, name, axis=0, tiled=True)  18.3 us
    dot_general x1, matrix products, body(): jnp.einsum('qhl,hlv->qhv', part_lat, w_uv, preferred_element_type=jnp.flo...  9.17 us
  transfers between devices with their start and end apart: 4, of which 4 were waited for; matrix products, arithmetic and copies ran while one was open for 2% of the time, Pallas kernels for 0%

profile of v2, /device:TPU:1, one launch (start us, length us, event | category | flops | bytes accessed | tf_op | source)
XLA Modules:
  0.0 309.4 jit_solution(3935303398965658325)
XLA Ops:
  6.5 0.0 copy-start
  6.5 0.8 pad_maximum_fusion.4
  7.4 8.3 %all_gather.27 = bf16[16,1536]{1,0:T(8,128)(2,1)S(1)} all-gather(bf16[8,1536]{1,0:T(8,128)(2,1)S(1)} %pad_maximum_fusion.4), channel_id=1, replica_groups=mesh['cz'=8,'cy'=4,'cc'=2,'wa'=8] {'cc'}, dimensions={0}, use_global_device_ids=true | all-gather | bytes 73728 | tf_op jit(solution)/shard_map/all_gather | solution.py:32
  15.7 10.0 %all_gather.28 = bf16[64,1536]{1,0:T(8,128)(2,1)} all-gather(bf16[16,1536]{1,0:T(8,128)(2,1)S(1)} %all_gather.27), channel_id=1, replica_groups=mesh['cz'=8,'cy'=4,'cc'=2,'wa'=8] {'cy'}, dimensions={0}, use_global_device_ids=true | all-gather | bytes 245760 | tf_op jit(solution)/shard_map/all_gather | solution.py:32
  25.7 0.0 all-gather.5.cloned.1.call-update
  25.7 0.0 reduce-scatter.4.cloned.1.call-start
  25.7 0.7 broadcast_in_dim.10
  26.5 0.1 reshape.110
  26.5 0.7 copy.42
  27.3 0.1 reduce
  27.4 1.5 copy.47
  28.9 0.2 convert_reduce_fusion.1
  29.1 0.1 convert_reduce_fusion
  29.2 0.3 fusion.23
  29.5 0.0 copy-start.2
  29.5 2.1 multiply_convert_fusion
  31.6 58.0 %all-gather.5.cloned.1.call-done = bf16[512,1536]{1,0:T(8,128)(2,1)} async-done(((bf16[64,1536]{1,0:T(8,128)(2,1)}), bf16[512,1536]{1,0:T(8,128)(2,1)}) %all-gather.5.cloned.1.call-update) | async-done | bytes 1572880 | tf_op jit(solution)/shard_map/all_gather | solution.py:32
  89.6 1.3 slice.39
  90.9 0.5 copy.59
  91.5 1.1 slice.40
  92.6 1.0 copy.46
  93.6 1.3 convert_bitcast_fusion
  95.0 4.7 %fusion = (f32[512,8]{0,1:T(8,128)S(1)}, f32[512,8,520]{0,2,1:T(8,128)S(1)}) fusion(pred[512,520]{0,1:T(8,128)(4,1)S(1)} %fusion.23, bf16[8,576]{0,1:T(8,128)(2,1)S(1)} %copy-done.5, bf16[512,576]{0,1:T(8,128)(2,1)S(1)} %copy-done.3, bf16[512,8,64]{0,2,1:T(8,128)(2,1)S(1)} %bitcast.37, bf16[512,8,512]{0,2,1:T(8,128)(2,1)S(1)} %convert_bitcast_fusion), kind=kOutput, calls=%fused_computation.2 | convolution fusion | flops 2470688768 | bytes 14119936 | tf_op jit(solution)/shard_map/qhl,kl->qhk/dot_general | solution.py:84
  99.7 0.0 copy-start.7
  99.7 3.2 %copy-done.1 = f32[512,8,520]{0,2,1:T(8,128)} copy-done((f32[512,8,520]{0,2,1:T(8,128)}, f32[512,8,520]{0,2,1:T(8,128)S(1)}, u32[]{:S(2)}) %copy-start.1) | copy-done | bytes 8519704
  102.9 1.7 fusion.1
  104.7 8.2 %all-gather = f32[1024,16]{0,1:T(8,128)S(1)} all-gather(f32[512,16]{0,1:T(8,128)S(1)} %pad_maximum_fusion.1), channel_id=2, replica_groups=mesh['cz'=8,'cy'=4,'cc'=2,'wa'=8] {'cc'}, dimensions={0}, use_global_device_ids=true | all-gather | bytes 98304 | tf_op jit(solution)/shard_map/all_gather | solution.py:44
  112.9 0.1 reshape.114
  113.0 0.1 fusion.33
  113.1 9.9 %all-gather.1 = f32[2048,16]{0,1:T(8,128)S(1)} all-gather(f32[512,16]{0,1:T(8,128)S(1)} %pad_maximum_fusion.2), channel_id=3, replica_groups=mesh['cz'=8,'cy'=4,'cc'=2,'wa'=8] {'cy'}, dimensions={0}, use_global_device_ids=true | all-gather | bytes 163840 | tf_op jit(solution)/shard_map/all_gather | solution.py:44
  123.0 0.1 reshape.115
  123.1 0.1 fusion.32
  123.2 40.8 %all-gather.2 = f32[4096,16]{0,1:T(8,128)S(1)} all-gather(f32[512,16]{0,1:T(8,128)S(1)} %pad_maximum_fusion.3), channel_id=4, replica_groups=mesh['cz'=8,'cy'=4,'cc'=2,'wa'=8] {'cz'}, dimensions={0}, use_global_device_ids=true | all-gather | bytes 294912 | tf_op jit(solution)/shard_map/all_gather | solution.py:44
  164.1 0.2 copy.60
  164.3 0.6 is-finite_select_fusion
  164.9 9.2 %bitcast_multiply_fusion = f32[512,8,128]{0,2,1:T(8,128)S(1)} fusion(bf16[8,512,128]{2,1,0:T(8,128)(2,1)} %param.12, f32[512,8,520]{0,2,1:T(8,128)} %copy-done.1, f32[512,8]{0,1:T(8,128)} %copy-done.7, pred[512,520]{0,1:T(8,128)(4,1)} %copy-done.2, f32[512,8]{0,1:T(8,128)} %get-tuple-element.6, bf16[512,576]{0,1:T(8,128)(2,1)} %multiply_convert_fusion, ...), kind=kOutput, calls=%fused_computation.17 | convolution fusion | flops 2730115072 | bytes 12563456 | tf_op jit(solution)/shard_map/qhl,hlv->qhv/dot_general | solution.py:95
  174.1 1.9 copy.51
  175.9 0.0 reduce-scatter.4.cloned.1.call-update
  176.0 0.0 reduce-scatter.6.cloned.1.call-start
  176.0 71.0 %reduce-scatter.4.cloned.1.call-done = f32[64,1024]{1,0:T(8,128)} async-done(((f32[512,1024]{1,0:T(8,128)}), f32[64,1024]{1,0:T(8,128)}) %reduce-scatter.4.cloned.1.call-update) | async-done | bytes 262160 | tf_op jit(solution)/shard_map/reduce_scatter | solution.py:38
  247.0 0.0 reduce-scatter.6.cloned.1.call-update
  247.1 0.0 reduce-scatter.8.cloned.1.call-start
  247.1 30.2 %reduce-scatter.6.cloned.1.call-done = f32[16,1024]{1,0:T(8,128)} async-done(((f32[64,1024]{1,0:T(8,128)}), f32[16,1024]{1,0:T(8,128)}) %reduce-scatter.6.cloned.1.call-update) | async-done | bytes 65552 | tf_op jit(solution)/shard_map/reduce_scatter | solution.py:38
  277.3 0.0 reduce-scatter.8.cloned.1.call-update
  277.3 0.1 fusion.31
  277.4 0.1 constant_dynamic-slice_fusion
  277.5 24.0 %reduce-scatter.8.cloned.1.call-done = f32[8,1024]{1,0:T(8,128)} async-done(((f32[16,1024]{1,0:T(8,128)}), f32[8,1024]{1,0:T(8,128)}) %reduce-scatter.8.cloned.1.call-update) | async-done | bytes 32784 | tf_op jit(solution)/shard_map/reduce_scatter | solution.py:38
  301.4 1.4 fusion.34
  (28 shorter events, 0.2 us)
Async XLA Ops:
  6.5 87.1 %copy-start = (bf16[8,128,512]{2,1,0:T(8,128)(2,1)S(1)}, bf16[8,128,512]{2,1,0:T(8,128)(2,1)}, u32[]{:S(2)}) copy-start(bf16[8,128,512]{2,1,0:T(8,128)(2,1)} %param.11) | copy-start | bytes 3145732
  6.5 83.1 %all-gather.5.cloned.1.call-start = ((), (), s32[]{:S(2)}) async-start(), calls=%async_computation.3 | async-start | bytes 1769472 | tf_op jit(solution)/shard_map/all_gather | solution.py:32
  25.7 221.4 %reduce-scatter.4.cloned.1.call-start = ((), (), s32[]{:S(2)}) async-start(), calls=%async_computation.4 | async-start | bytes 2359296 | tf_op jit(solution)/shard_map/reduce_scatter | solution.py:38
  29.5 70.2 %copy-start.2 = (pred[512,520]{0,1:T(8,128)(4,1)}, pred[512,520]{0,1:T(8,128)(4,1)S(1)}, u32[]{:S(2)}) copy-start(pred[512,520]{0,1:T(8,128)(4,1)S(1)} %fusion.23) | copy-start | bytes 798724
  91.5 3.5 %copy-start.3 = (bf16[512,576]{0,1:T(8,128)(2,1)S(1)}, bf16[512,576]{0,1:T(8,128)(2,1)}, u32[]{:S(2)}) copy-start(bf16[512,576]{0,1:T(8,128)(2,1)} %multiply_convert_fusion) | copy-start | bytes 1769476
  93.6 1.3 copy-start.4
  93.6 1.3 copy-start.5
  99.6 3.3 %copy-start.1 = (f32[512,8,520]{0,2,1:T(8,128)}, f32[512,8,520]{0,2,1:T(8,128)S(1)}, u32[]{:S(2)}) copy-start(f32[512,8,520]{0,2,1:T(8,128)S(1)} %get-tuple-element.8) | copy-start | bytes 25559044
  99.7 23.3 %copy-start.7 = (f32[512,8]{0,1:T(8,128)}, f32[512,8]{0,1:T(8,128)S(1)}, u32[]{:S(2)}) copy-start(f32[512,8]{0,1:T(8,128)S(1)} %is-finite_select_fusion.3) | copy-start | bytes 49156
  102.9 62.0 %copy-start.6 = (bf16[8,576]{0,1:T(8,128)(2,1)S(1)}, bf16[8,576]{0,1:T(8,128)(2,1)}, u32[]{:S(2)}) copy-start(bf16[8,576]{0,1:T(8,128)(2,1)} %copy.47) | copy-start | bytes 27652
  174.1 103.3 %copy-start.8 = (f32[512,8]{0,1:T(8,128)S(1)}, f32[512,8]{0,1:T(8,128)}, u32[]{:S(2)}) copy-start(f32[512,8]{0,1:T(8,128)} %get-tuple-element.5) | copy-start | bytes 49156
  176.0 101.3 %reduce-scatter.6.cloned.1.call-start = ((), (), s32[]{:S(2)}) async-start(), calls=%async_computation.5 | async-start | bytes 327680 | tf_op jit(solution)/shard_map/reduce_scatter | solution.py:38
  247.1 54.4 %reduce-scatter.8.cloned.1.call-start = ((), (), s32[]{:S(2)}) async-start(), calls=%async_computation.6 | async-start | bytes 98304 | tf_op jit(solution)/shard_map/reduce_scatter | solution.py:38
Sparse Core Ops, SparseCore 0:
  25.8 63.7 all-gather.4
  176.1 70.9 reduce-scatter.3
  249.9 27.3 reduce-scatter.5
  279.9 21.4 reduce-scatter.7

commit v3 on v2

v3 whole, which is shorter than its diff:
```python
import jax
import jax.numpy as jnp
import numpy as np
from jax import lax
from jax.sharding import Mesh, PartitionSpec as P

CHIP_PARTS = ("cz", "cy")
CORE = "cc"


def doc_index(position, new_lengths):
    ends = jnp.cumsum(new_lengths)
    return jnp.sum((ends[None, :] <= position[:, None]).astype(jnp.int32), axis=1)


def absorb_rows(nope_rows, w_uk):
    row_count = nope_rows.shape[0]
    heads_dev, nope_dim, latent_dim = w_uk.shape
    shaped = nope_rows.reshape(row_count, heads_dev, nope_dim)
    absorbed = jnp.einsum("thn,hnl->thl", shaped, w_uk, preferred_element_type=jnp.float32)
    return absorbed.astype(jnp.bfloat16)


def chip_index():
    index = lax.axis_index(CHIP_PARTS[0])
    for name in CHIP_PARTS[1:]:
        index = index * lax.axis_size(name) + lax.axis_index(name)
    return index


def gather_rows(x):
    for name in reversed(CHIP_PARTS):
        x = lax.all_gather(x, name, axis=0, tiled=True)
    return x


def scatter_rows(x):
    for name in CHIP_PARTS:
        x = lax.psum_scatter(x, name, scatter_dimension=0, tiled=True)
    return x


def merge_stats(stats, heads_dev):
    for name in reversed(CHIP_PARTS):
        group = lax.all_gather(stats, name, axis=0, tiled=False)
        peak = jnp.max(group[:, :, :heads_dev], axis=0)
        shifted = jnp.where(jnp.isfinite(peak), peak, jnp.zeros_like(peak))
        scale = jnp.exp(group[:, :, :heads_dev] - shifted[None])
        total = jnp.sum(scale * group[:, :, heads_dev:], axis=0)
        stats = jnp.concatenate([peak, total], axis=1)
    return stats[:, :heads_dev], stats[:, heads_dev:]


def swap_cores(x):
    return lax.ppermute(x, CORE, [(0, 1), (1, 0)])


def body(q_nope, q_rope, w_uk, w_uv, cache, cache_scale, new_latent, cache_doc, new_lengths):
    tok_rows = q_nope.shape[0]
    heads_dev, nope_dim, latent_dim = w_uk.shape
    value_dim = w_uv.shape[2]
    rope_dim = q_rope.shape[1] // heads_dev
    cores = lax.axis_size(CORE)
    chips = 1
    for name in CHIP_PARTS:
        chips = chips * lax.axis_size(name)
    q_rows = tok_rows * chips
    my_chip = chip_index()
    my_core = lax.axis_index(CORE)
    other_core = 1 - my_core
    score_scale = (nope_dim + rope_dim) ** (-0.5)

    dequant = (cache.astype(jnp.float32) * cache_scale[:, None]).astype(jnp.bfloat16)
    own_keys = jnp.concatenate([dequant, new_latent], axis=0)
    other_keys = swap_cores(own_keys)
    other_doc = swap_cores(cache_doc)

    own_q = jnp.concatenate([q_nope, q_rope], axis=1)
    all_q = gather_rows(own_q)
    nope_width = heads_dev * nope_dim
    all_lat = absorb_rows(all_q[:, :nope_width], w_uk)
    all_rope = all_q[:, nope_width:]
    query = jnp.concatenate(
        [all_lat, all_rope.reshape(q_rows, heads_dev, rope_dim)],
        axis=2,
    )
    cache_len = cache.shape[0]
    block_len = cache_len // cache_doc.shape[0]
    row = jnp.arange(q_rows, dtype=jnp.int32)
    query_pos = ((row // tok_rows) * cores + my_core) * tok_rows + row % tok_rows
    query_doc = doc_index(query_pos, new_lengths)

    def key_meta(core, docs):
        new_pos = (my_chip * cores + core) * tok_rows + jnp.arange(tok_rows, dtype=jnp.int32)
        key_doc = jnp.concatenate([jnp.repeat(docs, block_len), doc_index(new_pos, new_lengths)])
        key_pos = jnp.concatenate([jnp.full((cache_len,), -1, dtype=jnp.int32), new_pos])
        return key_doc, key_pos

    own_doc, own_pos = key_meta(my_core, cache_doc)
    far_doc, far_pos = key_meta(other_core, other_doc)
    key_rows = jnp.concatenate([own_keys, other_keys], axis=0)
    key_doc = jnp.concatenate([own_doc, far_doc])
    key_pos = jnp.concatenate([own_pos, far_pos])
    allowed = (query_doc[:, None] == key_doc[None, :]) & (key_pos[None, :] <= query_pos[:, None])
    score = (
        jnp.einsum("qhl,kl->qhk", query, key_rows, preferred_element_type=jnp.float32) * score_scale
    )
    masked = jnp.where(allowed[:, None, :], score, -jnp.inf)
    local_max = jnp.max(masked, axis=2)
    shift = jnp.where(jnp.isfinite(local_max), local_max, jnp.zeros_like(local_max))
    weight = jnp.exp(masked - shift[:, :, None])
    totals = jnp.sum(weight, axis=2)
    weight_low = weight.astype(jnp.bfloat16)
    part_lat = jnp.einsum(
        "qhk,kl->qhl", weight_low, key_rows[:, :latent_dim], preferred_element_type=jnp.float32
    ).astype(jnp.bfloat16)
    numerator = jnp.einsum("qhl,hlv->qhv", part_lat, w_uv, preferred_element_type=jnp.float32)
    row_max, row_total = merge_stats(jnp.concatenate([local_max, totals], axis=1), heads_dev)
    factor = jnp.exp(local_max - row_max)
    scaled = (numerator * factor[:, :, None]).reshape(q_rows, heads_dev * value_dim)
    own_numer = scatter_rows(scaled).reshape(tok_rows, heads_dev, value_dim)
    own_total = lax.dynamic_slice_in_dim(row_total, my_chip * tok_rows, tok_rows, axis=0)
    result = own_numer / own_total[:, :, None]
    return result.astype(jnp.bfloat16).reshape(tok_rows, heads_dev * value_dim)


def solution(mesh):
    ctx_shape = (8, 4, 2)
    grid = np.asarray(mesh.devices).reshape(ctx_shape + (mesh.shape["wa"],))
    fine = Mesh(grid, CHIP_PARTS + (CORE, "wa"))
    rows = CHIP_PARTS + (CORE,)
    placed = (
        P(rows, "wa"),
        P(rows, "wa"),
        P("wa", None, None),
        P("wa", None, None),
        P(rows, None),
        P(rows),
        P(rows, None),
        P(rows),
        P(),
    )
    return jax.shard_map(
        body, mesh=fine, in_specs=placed, out_specs=P(rows, "wa"), check_vma=False
    )
```

time: 310 us -> 269 us (0.87)
  waiting for transfers between devices: 183 us -> 108 us
  blocking collectives: 77.2 us -> 101 us
  starting transfers between devices: 0.12 us -> 10.9 us
    all_gather x1 -> x0, waiting for transfers between devices: 58 us -> none  [gather_rows(): x = lax.all_gather(x, name, axis=0, tiled=True)]
    all_gather x2, blocking collectives: 18.3 us -> 51.8 us  [gather_rows(): x = lax.all_gather(x, name, axis=0, tiled=True)]
    reduce_scatter x3 -> x2, waiting for transfers between devices: 125 us -> 108 us  [scatter_rows(): x = lax.psum_scatter(x, name, scatter_dimension=0, tiled=True)]
    ppermute x0 -> x2, starting transfers between devices: none -> 10.8 us  [swap_cores(): return lax.ppermute(x, CORE, [(0, 1), (1, 0)])]
    all_gather x3 -> x2, blocking collectives: 58.9 us -> 49.2 us  [merge_stats(): group = lax.all_gather(stats, name, axis=0, tiled=False)]
    concatenate x1 -> x4, local copies, waits for them, and re-layouts: 0.01 us -> 3.37 us  [the longest x1 2.06 us: body(): key_rows = jnp.concatenate([own_keys, other_keys], axis=0)]
  transfers between devices with their start and end apart: 4 -> 4, of which waited for: 4 -> 2; matrix products, arithmetic and copies ran while one was open for 2% -> 3% of each run, Pallas kernels for 0% -> 0%
where the time goes in v3:
time: 269 us; the launch traced here: 267 us
  waiting for transfers between devices  108 us (40%)
  blocking collectives  101 us (38%)
  matrix products  16.7 us (6%)
  between operations  13.7 us (5%)
  local copies, waits for them, and re-layouts  11.1 us (4%)
  starting transfers between devices  10.9 us (4%)
  other arithmetic  5.83 us (2%)
    reduce_scatter x2, waiting for transfers between devices, scatter_rows(): x = lax.psum_scatter(x, name, scatter_dimension=0, tiled=True)  108 us
    all_gather x2, blocking collectives, gather_rows(): x = lax.all_gather(x, name, axis=0, tiled=True)  51.8 us
    all_gather x2, blocking collectives, merge_stats(): group = lax.all_gather(stats, name, axis=0, tiled=False)  49.2 us
    ppermute x2, starting transfers between devices, swap_cores(): return lax.ppermute(x, CORE, [(0, 1), (1, 0)])  10.8 us
    dot_general x1, matrix products, body(): jnp.einsum('qhl,hlv->qhv', part_lat, w_uv, preferred_element_type=jnp.flo...  8.42 us
    dot_general x1, matrix products, body(): jnp.einsum('qhl,kl->qhk', query, key_rows, preferred_element_type=jnp.flo...  6.19 us
  transfers between devices with their start and end apart: 4, of which 2 were waited for; matrix products, arithmetic and copies ran while one was open for 3% of the time, Pallas kernels for 0%

profile of v3, /device:TPU:1, one launch (start us, length us, event | category | flops | bytes accessed | tf_op | source)
XLA Modules:
  0.0 266.9 jit_solution(17568479425091766491)
XLA Ops:
  6.5 0.0 copy-start
  6.5 0.0 reduce-scatter.3.cloned.1.call-start
  6.6 8.9 %collective-permute-start = (s32[8]{0:T(128)}, s32[8]{0:T(128)S(1)}, u32[]{:S(2)}, u32[]{:S(2)}) collective-permute-start(s32[8]{0:T(128)} %param.16), channel_id=1, source_target_pairs={{0,8},{8,0},{1,9},{9,1},{2,10},{10,2},{3,11},{11,3},{4,12},{12,4},... | collective-permute-start | bytes 104 | tf_op jit(solution)/shard_map/ppermute | solution.py:55
  15.5 0.9 copy.64
  16.4 1.2 multiply_convert_fusion
  17.6 0.1 pad_maximum_fusion
  17.7 1.1 copy.63
  18.8 1.9 collective-permute-start.1
  20.8 0.1 copy.57
  20.9 0.1 reduce
  21.0 0.0 copy-done.6
  21.0 9.0 %all_gather.18 = bf16[32,1536]{1,0:T(8,128)(2,1)S(1)} all-gather(bf16[8,1536]{1,0:T(8,128)(2,1)S(1)} %pad_maximum_fusion.1), channel_id=1, replica_groups=mesh['cz'=8,'cy'=4,'cc'=2,'wa'=8] {'cy'}, dimensions={0}, use_global_device_ids=true | all-gather | bytes 122880 | tf_op jit(solution)/shard_map/all_gather | solution.py:33
  30.1 42.8 %all_gather.19 = bf16[256,1536]{1,0:T(8,128)(2,1)S(1)} all-gather(bf16[32,1536]{1,0:T(8,128)(2,1)S(1)} %all_gather.18), channel_id=1, replica_groups=mesh['cz'=8,'cy'=4,'cc'=2,'wa'=8] {'cz'}, dimensions={0}, use_global_device_ids=true | all-gather | bytes 884736 | tf_op jit(solution)/shard_map/all_gather | solution.py:33
  72.9 0.1 slice.30
  72.9 0.0 copy-start.8
  72.9 0.2 copy.75
  73.1 0.1 convert_reduce_fusion
  73.2 2.1 convert_bitcast_fusion
  75.4 0.0 copy-done.8
  75.4 0.1 broadcast_in_dim.12
  75.4 0.1 reshape.143
  75.5 0.1 copy.76
  75.7 0.3 copy.61
  76.0 0.1 concatenate.26
  76.1 0.2 convert_reduce_fusion.1
  76.3 0.0 collective-permute-done
  76.3 0.1 broadcast_in_dim.13
  76.4 0.1 reshape.144
  76.5 0.1 concatenate.25
  76.5 0.7 compare_and_fusion
  77.3 0.0 collective-permute-done.1
  77.3 1.4 copy.65
  78.7 2.1 concatenate.30
  80.8 6.2 %fusion = (f32[256,8]{0,1:T(8,128)S(1)}, f32[256,8,1040]{0,2,1:T(8,128)S(1)}) fusion(pred[256,1040]{0,1:T(8,128)(4,1)S(1)} %compare_and_fusion, bf16[1040,576]{0,1:T(8,128)(2,1)} %concatenate.30, bf16[256,8,64]{2,0,1:T(8,128)(2,1)S(1)} %copy.61, bf16[256,8,512]{2,0,1:T(8,128)(2,1)} %convert_bitcast_fusion), kind=kOutput, calls=%fused_computation.2 | convolution fusion | flops 2464774144 | bytes 12351488 | tf_op jit(solution)/shard_map/qhl,kl->qhk/dot_general | solution.py:106
  87.0 0.0 copy-start.1
  87.0 1.7 fusion.1
  88.8 1.5 copy-done.1
  90.3 9.0 %all-gather = f32[1024,16]{0,1:T(8,128)S(1)} all-gather(f32[256,16]{0,1:T(8,128)S(1)} %pad_maximum_fusion.2), channel_id=2, replica_groups=mesh['cz'=8,'cy'=4,'cc'=2,'wa'=8] {'cy'}, dimensions={0}, use_global_device_ids=true | all-gather | bytes 81920 | tf_op jit(solution)/shard_map/all_gather | solution.py:45
  99.4 40.3 %all-gather.1 = f32[2048,16]{0,1:T(8,128)S(1)} all-gather(f32[256,16]{0,1:T(8,128)S(1)} %pad_maximum_fusion.3), channel_id=3, replica_groups=mesh['cz'=8,'cy'=4,'cc'=2,'wa'=8] {'cz'}, dimensions={0}, use_global_device_ids=true | all-gather | bytes 147456 | tf_op jit(solution)/shard_map/all_gather | solution.py:45
  139.8 8.4 %fusion.24 = f32[256,8,128]{0,2,1:T(8,128)} fusion(bf16[8,512,128]{2,1,0:T(8,128)(2,1)} %param.12, f32[256,8,1040]{0,2,1:T(8,128)} %copy-done.1, f32[256,8]{0,1:T(8,128)S(1)} %is-finite_select_fusion.2, pred[256,1040]{0,1:T(8,128)(4,1)S(1)} %compare_and_fusion, bf16[1040,576]{0,1:T(8,128)(2,1)S(1)} %copy-done.4, f32[256,8]{0,1:T(8,128)S(1)} %get-tuple-element.8), kind=kOutput, calls=%fused_computation.18 | convolution fusion | flops 2459303936 | bytes 12079104 | tf_op jit(solution)/shard_map/qhl,hlv->qhv/dot_general | solution.py:117
  148.2 2.5 copy.69
  150.8 0.0 reduce-scatter.3.cloned.1.call-update
  150.8 0.0 reduce-scatter.5.cloned.1.call-start
  150.8 79.8 %reduce-scatter.3.cloned.1.call-done = f32[32,1024]{1,0:T(8,128)} async-done(((f32[256,1024]{1,0:T(8,128)}), f32[32,1024]{1,0:T(8,128)}) %reduce-scatter.3.cloned.1.call-update) | async-done | bytes 131088 | tf_op jit(solution)/shard_map/reduce_scatter | solution.py:39
  230.7 0.0 reduce-scatter.5.cloned.1.call-update
  230.7 0.1 constant_dynamic-slice_fusion
  230.8 27.8 %reduce-scatter.5.cloned.1.call-done = f32[8,1024]{1,0:T(8,128)} async-done(((f32[32,1024]{1,0:T(8,128)}), f32[8,1024]{1,0:T(8,128)}) %reduce-scatter.5.cloned.1.call-update) | async-done | bytes 32784 | tf_op jit(solution)/shard_map/reduce_scatter | solution.py:39
  258.6 1.4 fusion.32
  (29 shorter events, 0.3 us)
Async XLA Ops:
  6.5 66.7 %copy-start = (bf16[8,128,512]{2,1,0:T(8,128)(2,1)S(1)}, bf16[8,128,512]{2,1,0:T(8,128)(2,1)}, u32[]{:S(2)}) copy-start(bf16[8,128,512]{2,1,0:T(8,128)(2,1)} %param.11) | copy-start | bytes 3145732
  6.5 14.2 %copy-start.7 = (s32[16]{0:T(128)S(1)}, s32[16]{0:T(128)}, u32[]{:S(2)}) copy-start(s32[16]{0:T(128)} %param.17) | copy-start | bytes 196
  6.5 14.5 %copy-start.6 = (bf16[8,512]{1,0:T(8,128)(2,1)S(1)}, bf16[8,512]{1,0:T(8,128)(2,1)}, u32[]{:S(2)}) copy-start(bf16[8,512]{1,0:T(8,128)(2,1)} %param.10) | copy-start | bytes 24580
  6.5 14.5 %copy-start.5 = (bf16[8,1024]{1,0:T(8,128)(2,1)S(1)}, bf16[8,1024]{1,0:T(8,128)(2,1)}, u32[]{:S(2)}) copy-start(bf16[8,1024]{1,0:T(8,128)(2,1)} %param.9) | copy-start | bytes 49156
  6.5 224.1 %reduce-scatter.3.cloned.1.call-start = ((), (), s32[]{:S(2)}) async-start(), calls=%async_computation.2 | async-start | bytes 1179648 | tf_op jit(solution)/shard_map/reduce_scatter | solution.py:39
  6.6 69.7 %collective-permute-start = (s32[8]{0:T(128)}, s32[8]{0:T(128)S(1)}, u32[]{:S(2)}, u32[]{:S(2)}) collective-permute-start(s32[8]{0:T(128)} %param.16), channel_id=1, source_target_pairs={{0,8},{8,0},{1,9},{9,1},{2,10},{10,2},{3,11},{11,3},{4,12},{12,4},... | collective-permute-start | bytes 104 | tf_op jit(solution)/shard_map/ppermute | solution.py:55
  16.3 4.7 %copy-start.2 = (bf16[8,576]{0,1:T(8,128)(2,1)}, bf16[8,576]{0,1:T(8,128)(2,1)S(1)}, u32[]{:S(2)}) copy-start(bf16[8,576]{0,1:T(8,128)(2,1)S(1)} %copy.64) | copy-start | bytes 27652
  18.8 58.5 %collective-permute-start.1 = (bf16[520,576]{1,0:T(8,128)(2,1)}, bf16[520,576]{1,0:T(8,128)(2,1)}, u32[]{:S(2)}, u32[]{:S(2)}) collective-permute-start(bf16[520,576]{1,0:T(8,128)(2,1)} %copy.63), channel_id=1, source_target_pairs={{0,8},{8,0},{1,9},{9,1},{2,10},{10,2},{3,11},{11,3},{4,12},{12,4},... | collective-permute-start | bytes 1797128 | tf_op jit(solution)/shard_map/ppermute | solution.py:55
  72.9 2.4 copy-start.8
  75.3 3.4 %copy-start.3 = (bf16[8,576]{0,1:T(8,128)(2,1)S(1)}, bf16[8,576]{0,1:T(8,128)(2,1)}, u32[]{:S(2)}) copy-start(bf16[8,576]{0,1:T(8,128)(2,1)} %copy-done.2) | copy-start | bytes 27652
  87.0 3.3 %copy-start.1 = (f32[256,8,1040]{0,2,1:T(8,128)}, f32[256,8,1040]{0,2,1:T(8,128)S(1)}, u32[]{:S(2)}) copy-start(f32[256,8,1040]{0,2,1:T(8,128)S(1)} %get-tuple-element.10) | copy-start | bytes 25559044
  87.0 52.8 %copy-start.4 = (bf16[1040,576]{0,1:T(8,128)(2,1)S(1)}, bf16[1040,576]{0,1:T(8,128)(2,1)}, u32[]{:S(2)}) copy-start(bf16[1040,576]{0,1:T(8,128)(2,1)} %concatenate.30) | copy-start | bytes 3594244
  150.8 107.8 %reduce-scatter.5.cloned.1.call-start = ((), (), s32[]{:S(2)}) async-start(), calls=%async_computation.3 | async-start | bytes 163840 | tf_op jit(solution)/shard_map/reduce_scatter | solution.py:39
Sparse Core Ops, SparseCore 0:
  150.9 79.7 reduce-scatter.2
  233.5 25.1 reduce-scatter.4
